TPU v7x, 128 devices: a whole 4x4x4 slice. The times are simulated.
128 devices in a mesh: shot: 16 (over z, x_lo, core), brick: 8 (over y, x_hi).
Axes of the slice: x: 4 (x_hi: 2, x_lo: 2; x = x_hi * 2 + x_lo), y: 4, z: 4, core: 2. Of those that a mesh axis runs over, the one named last changes fastest.
Arguments:
- sources: float32 [16, 2, 2, 256, 64, 256], P('shot', None, None, None, 'brick'), may hold values from -24 to 24
- slowness: float32 [16, 256, 64, 256], P('shot', None, 'brick'), may hold values from 0.5 to 2
- group_size: int32 [16], replicated, may hold values from 2 to 8, as said below
- window_anchor: int32 [16], replicated, may hold values from 0 to 56
- tile_slot: int32 [64], replicated, may hold values from 0 to 63, each once
Outputs:
- gradient: float32 [8, 64, 65536], P('brick', 'shot')
Inputs may be any that keep to these rules, and one draw needn't show every extreme that they name: `group_size`: some shot spans all 8 bricks and some shot only 2. Window s covers model tiles window_anchor[s] to window_anchor[s] + 7. `tile_slot`: each slot of 0 to 63 once.
All inputs are finite; a program needn't handle non-finite values.
Results may differ from a plain program's by a relative error of at most 0.0003.
Values sent between devices are 32-bit elements; how exact they have to be, the bound alone decides.
No kernel may reach another device: no remote copies, remote signals or barrier semaphores. Data moves between devices by JAX's collectives and lax.ppermute only.
A program may use at most 128 MiB of HBM per device.

v0:
```python
import jax
import jax.numpy as jnp
from jax import lax
from jax.sharding import PartitionSpec as P

BLOCKS = 8
shift_beta = 0.5
relaxation = 0.8


def extended(value, sides, width):
    for axis, dim in sides:
        size, length = (lax.axis_size(axis), value.shape[dim])
        up = [(i, (i + 1) % size) for i in range(size - 1)]
        down = [(j, i) for i, j in up]
        last = lax.slice_in_dim(value, length - width, length, axis=dim)
        first = lax.slice_in_dim(value, 0, width, axis=dim)
        before = lax.ppermute(last, axis, up)
        after = lax.ppermute(first, axis, down)
        value = jnp.concatenate([before, value, after], axis=dim)
    return value


def lateral_sum(field):
    summed = jnp.zeros_like(field)
    for along_axis in (1, 3):
        widths = [(0, 0)] * 4
        widths[along_axis] = (1, 1)
        padded = jnp.pad(field, widths)
        count = field.shape[along_axis]
        summed = summed + lax.slice_in_dim(padded, 0, count, axis=along_axis)
        summed = summed + lax.slice_in_dim(padded, 2, count + 2, axis=along_axis)
    return summed


def apply_inverse(values, inv_re, inv_im):
    fwd_re = values[0] * inv_re - values[1] * inv_im
    fwd_im = values[0] * inv_im + values[1] * inv_re
    adj_re = values[2] * inv_re - values[3] * inv_im
    adj_im = values[2] * inv_im + values[3] * inv_re
    return jnp.stack([fwd_re, fwd_im, adj_re, adj_im])


def sine_taper(count, extent):
    positions = jnp.arange(count, dtype=jnp.int32).astype(jnp.float32)
    return jnp.sin(jnp.pi * (positions + 0.5) / extent)


def per_device(sources, slowness, group_size, window_anchor, tile_slot):
    slowness_window = slowness[0]
    wide_y, planes, wide_z = slowness_window.shape
    brick_index = lax.axis_index("brick")
    shot_index = lax.axis_index("shot")
    extent = group_size[shot_index] * planes
    depth_ids = brick_index * planes + jnp.arange(planes, dtype=jnp.int32)
    active = depth_ids < extent
    active_mask = active.astype(jnp.float32)[None, :, None]
    real_d = 6.0 - slowness_window
    imag_d = shift_beta * slowness_window
    denominator = real_d * real_d + imag_d * imag_d
    inv_re = real_d / denominator
    inv_im = imag_d / denominator
    forcing = sources[0].reshape(4, wide_y, planes, wide_z)
    field = relaxation * apply_inverse(forcing, inv_re, inv_im) * active_mask
    padded = extended(field, (("brick", 2),), 1)
    neighbours = padded[:, :, :-2, :] + padded[:, :, 2:, :] + lateral_sum(field)
    updated = apply_inverse(forcing + neighbours, inv_re, inv_im)
    field = ((1.0 - relaxation) * field + relaxation * updated) * active_mask
    imaging = (
        field[0] * field[2]
        - field[1] * field[3]
        - shift_beta * (field[0] * field[3] + field[1] * field[2])
    )
    extent_float = extent.astype(jnp.float32)
    depth_float = depth_ids.astype(jnp.float32)
    taper_x = jnp.where(active, jnp.sin(jnp.pi * (depth_float + 0.5) / extent_float), 0.0)
    taper_y = sine_taper(wide_y, float(wide_y))
    taper_z = sine_taper(wide_z, float(wide_z))
    gradient = imaging * (taper_y[:, None, None] * taper_x[None, :, None] * taper_z[None, None, :])
    blocks = gradient.reshape(BLOCKS, -1)
    shot_count = lax.axis_size("shot")
    tile_dev = tile_slot.shape[0] // shot_count
    owned = shot_index * tile_dev + jnp.arange(tile_dev, dtype=jnp.int32)
    piece_slots = tile_slot[window_anchor[:, None] + jnp.arange(BLOCKS, dtype=jnp.int32)[None, :]]
    weights = (owned[:, None, None] == piece_slots[None, :, :]).astype(jnp.float32)
    summed = jnp.einsum(
        "qkb,kbc->qc",
        weights,
        lax.all_gather(blocks[None], "shot", axis=0, tiled=True),
        precision=lax.Precision.HIGHEST,
    )
    return summed[None]


def solution(mesh):
    return jax.shard_map(
        per_device,
        mesh=mesh,
        in_specs=(
            P("shot", None, None, None, "brick", None),
            P("shot", None, "brick", None),
            P(),
            P(),
            P(),
        ),
        out_specs=P("brick", "shot", None),
        check_vma=False,
    )
```

profile of v0, /device:TPU:1, one launch (start us, length us, event | category | flops | bytes accessed | tf_op | source)
XLA Modules:
  0.0 342.5 jit_solution(932084848076161260)
XLA Ops:
  6.5 1.2 dynamic_slice.3
  8.4 9.2 %copy.14 = f32[1,2,2,256,8,256]{5,3,4,2,1,0:T(8,128)} copy(f32[1,2,2,256,8,256]{5,4,3,2,1,0:T(8,128)} %param.5) | data formatting | bytes 16777216 | tf_op args[0]
  17.7 5.0 %multiply_subtract_fusion.4 = (f32[1,256,8,256]{3,1,2,0:T(8,128)S(1)}, f32[1,256,8,256]{3,1,2,0:T(8,128)S(1)}, f32[1,256,8,256]{3,1,2,0:T(8,128)S(1)}, f32[1,256,8,256]{3,1,2,0:T(8,128)S(1)}) fusion(f32[4,256,8,256]{3,1,2,0:T(8,128)} %bitcast.10, f32[1,256,8,256]{3,2,1,0:T(8,128)} %param.6), kind=kLoop, calls=%fused_computation.24 | loop fusion | flops 9961472 | bytes 18874368 | tf_op jit(solution)/shard_map/sub | solution.py:37
  22.7 1.0 maximum_multiply_fusion
  24.2 0.6 copy-done.4
  25.3 3.2 copy-done.1
  28.5 1.2 fusion.15
  29.7 6.5 %collective-permute-start = (f32[4,256,1,256]{3,1,2,0:T(8,128)}, f32[4,256,1,256]{3,1,2,0:T(8,128)}, u32[]{:S(2)}, u32[]{:S(2)}) collective-permute-start(f32[4,256,1,256]{3,1,2,0:T(8,128)} %get-tuple-element.13), channel_id=1, source_target_pairs={{0,1},{1,2},{2,3},{3,4},{4,5},{5,6},{6,7},{8,9},{9,10},{10,11},{11... | collective-permute-start | bytes 3145736 | tf_op jit(solution)/shard_map/ppermute | solution.py:18
  36.2 1.3 collective-permute-start.1
  37.6 1.7 broadcast_multiply_fusion
  39.4 3.3 mul.300
  42.7 14.6 %collective-permute-done = f32[4,256,1,256]{3,1,2,0:T(8,128)} collective-permute-done((f32[4,256,1,256]{3,1,2,0:T(8,128)}, f32[4,256,1,256]{3,1,2,0:T(8,128)}, u32[]{:S(2)}, u32[]{:S(2)}) %collective-permute-start) | collective-permute-done | bytes 1048608 | tf_op jit(solution)/shard_map/ppermute | solution.py:18
  57.3 24.4 %collective-permute-done.1 = f32[4,256,1,256]{3,1,2,0:T(8,128)} collective-permute-done((f32[4,256,1,256]{3,1,2,0:T(8,128)S(1)}, f32[4,256,1,256]{3,1,2,0:T(8,128)}, u32[]{:S(2)}, u32[]{:S(2)}) %collective-permute-start.1) | collective-permute-done | bytes 1048608 | tf_op jit(solution)/shard_map/ppermute | solution.py:19
  81.8 23.0 %fusion.4 = f32[4,256,8,256]{3,1,2,0:T(8,128)S(1)} fusion(f32[4,256,8,256]{3,1,2,0:T(8,128)} %copy-done.1, f32[4,256,1,256]{3,1,2,0:T(8,128)} %collective-permute-done.1, f32[4,256,1,256]{3,1,2,0:T(8,128)} %collective-permute-done, f32[1,2,2,256,8,256]{5,3,4,2,1,0:T(8,128)} %copy.14), kind=kLoop, calls=%fused_computation.8 | loop fusion | flops 16777216 | bytes 27262976 | tf_op jit(solution)/shard_map/add | solution.py:67
  104.8 3.9 %multiply_subtract_fusion.2 = (f32[1,256,8,256]{3,1,2,0:T(8,128)S(1)}, f32[1,256,8,256]{3,1,2,0:T(8,128)}, f32[1,256,8,256]{3,1,2,0:T(8,128)}, f32[1,256,8,256]{3,1,2,0:T(8,128)}) fusion(f32[4,256,8,256]{3,1,2,0:T(8,128)S(1)} %fusion.4, f32[1,256,8,256]{3,2,1,0:T(8,128)S(1)} %copy-done.8), kind=kLoop, calls=%fused_computation.20 | loop fusion | flops 9961472 | bytes 18874368 | tf_op jit(solution)/shard_map/sub | solution.py:37
  108.8 1.1 copy-done.7
  109.9 4.2 %fusion.7 = f32[4,256,8,256]{3,1,2,0:T(8,128)S(1)} fusion(f32[1,256,8,256]{3,1,2,0:T(8,128)} %get-tuple-element.7, f32[1,256,8,256]{3,1,2,0:T(8,128)} %get-tuple-element.6, f32[1,256,8,256]{3,1,2,0:T(8,128)} %get-tuple-element.8, f32[1,256,8,256]{3,1,2,0:T(8,128)S(1)} %get-tuple-element.5, f32[8]{0:T(128)S(1)} %fusion.14, f32[8]{0:T(128)S(1)} %get-tuple-element.16, ...), kind=kLoop, calls=%fused_computation.15 | loop fusion | flops 23068672 | bytes 25165888 | tf_op jit(solution)/shard_map/mul | solution.py:68
  114.7 2.5 copy.17
  117.2 3.4 %sub.62 = f32[1,8,65536]{2,1,0:T(8,128)} reshape(f32[1,256,8,256]{3,2,1,0:T(8,128)} %copy.17) | data formatting | bytes 4194304 | tf_op jit(solution)/shard_map/sub | solution.py:70
  120.6 3.3 mul.301
  124.0 0.6 copy-done.10
  124.8 1.2 gather_fusion
  126.2 172.0 %all-gather.2.cloned.1.call-done = f32[16,8,65536]{2,1,0:T(8,128)} async-done(((f32[1,8,65536]{2,1,0:T(8,128)}), f32[16,8,65536]{2,1,0:T(8,128)}) %all-gather.2.cloned.1.call-update) | async-done | bytes 33554448 | tf_op jit(solution)/shard_map/all_gather | solution.py:89
  298.1 37.6 %convolution_bitcast_fusion = f32[1,4,65536]{2,1,0:T(4,128)} fusion(f32[16,8,65536]{2,1,0:T(8,128)} %all-gather.2.cloned.1.call-done, s32[16,8]{0,1:T(8,128)S(1)} %copy.13, s32[4]{0:T(128)S(1)} %iota_add_fusion.1), kind=kOutput, calls=%fused_computation.1 | convolution fusion | flops 402653696 | bytes 34603536 | tf_op jit(solution)/shard_map/qkb,kbc->qc/dot_general | solution.py:86
  (31 shorter events, 2.1 us)
Async XLA Ops:
  6.5 118.2 %copy-start = (s32[64]{0:T(128)S(1)}, s32[64]{0:T(128)}, u32[]{:S(2)}) copy-start(s32[64]{0:T(128)} %param.9) | copy-start | bytes 772
  6.5 291.6 %all-gather.2.cloned.1.call-start = ((), (), s32[]{:S(2)}) async-start(), calls=%async_computation | async-start | bytes 35651584 | tf_op jit(solution)/shard_map/all_gather | solution.py:89
  22.7 1.5 copy-start.2
  22.7 2.0 copy-start.4
  22.7 2.6 copy-start.6
  25.3 3.2 copy-start.1
  29.7 27.6 %collective-permute-start = (f32[4,256,1,256]{3,1,2,0:T(8,128)}, f32[4,256,1,256]{3,1,2,0:T(8,128)}, u32[]{:S(2)}, u32[]{:S(2)}) collective-permute-start(f32[4,256,1,256]{3,1,2,0:T(8,128)} %get-tuple-element.13), channel_id=1, source_target_pairs={{0,1},{1,2},{2,3},{3,4},{4,5},{5,6},{6,7},{8,9},{9,10},{10,11},{11... | collective-permute-start | bytes 3145736 | tf_op jit(solution)/shard_map/ppermute | solution.py:18
  36.2 45.6 %collective-permute-start.1 = (f32[4,256,1,256]{3,1,2,0:T(8,128)S(1)}, f32[4,256,1,256]{3,1,2,0:T(8,128)}, u32[]{:S(2)}, u32[]{:S(2)}) collective-permute-start(f32[4,256,1,256]{3,1,2,0:T(8,128)S(1)} %get-tuple-element.14), channel_id=1, source_target_pairs={{1,0},{2,1},{3,2},{4,3},{5,4},{6,5},{7,6},{9,8},{10,9},{11,10},{12... | collective-permute-start | bytes 3145736 | tf_op jit(solution)/shard_map/ppermute | solution.py:19
  42.7 62.1 %copy-start.8 = (f32[1,256,8,256]{3,2,1,0:T(8,128)S(1)}, f32[1,256,8,256]{3,2,1,0:T(8,128)}, u32[]{:S(2)}) copy-start(f32[1,256,8,256]{3,2,1,0:T(8,128)} %param.6) | copy-start | bytes 6291460
  104.8 4.0 %copy-start.3 = (f32[1,256,8,256]{3,1,2,0:T(8,128)S(1)}, f32[1,256,8,256]{3,1,2,0:T(8,128)}, u32[]{:S(2)}) copy-start(f32[1,256,8,256]{3,1,2,0:T(8,128)} %copy-done.2) | copy-start | bytes 6291460
  104.8 4.0 %copy-start.5 = (f32[1,256,8,256]{3,1,2,0:T(8,128)S(1)}, f32[1,256,8,256]{3,1,2,0:T(8,128)}, u32[]{:S(2)}) copy-start(f32[1,256,8,256]{3,1,2,0:T(8,128)} %copy-done.4) | copy-start | bytes 6291460
  104.8 5.1 %copy-start.7 = (f32[1,256,8,256]{3,1,2,0:T(8,128)S(1)}, f32[1,256,8,256]{3,1,2,0:T(8,128)}, u32[]{:S(2)}) copy-start(f32[1,256,8,256]{3,1,2,0:T(8,128)} %copy-done.6) | copy-start | bytes 6291460
  117.2 3.4 %copy-start.9 = (f32[1,8,65536]{2,1,0:T(8,128)S(1)}, f32[1,8,65536]{2,1,0:T(8,128)}, u32[]{:S(2)}) copy-start(f32[1,8,65536]{2,1,0:T(8,128)} %mul.300) | copy-start | bytes 6291460
  123.9 0.7 copy-start.10
Sparse Core Ops, SparseCore 0:
  124.1 174.0 all-gather.1
where the time goes:
time: 343 us
  waiting for transfers between devices  211 us (62%)
  other arithmetic  43.1 us (13%)
  matrix products  37.6 us (11%)
  local copies, waits for them, and re-layouts  28.9 us (8%)
  between operations  14.2 us (4%)
  starting transfers between devices  7.77 us (2%)
    all_gather x1, waiting for transfers between devices, per_device(): lax.all_gather(blocks[None], 'shot', axis=0, tiled=True)  172 us
    dot_general x1, matrix products, per_device(): jnp.einsum('qkb,kbc->qc', weights, lax.all_gather(blocks[None], 'shot', a...  37.6 us
    ppermute x1, waiting for transfers between devices, extended(): after = lax.ppermute(first, axis, down)  24.4 us
    add x1, other arithmetic, per_device(): updated = apply_inverse(forcing + neighbours, inv_re, inv_im)  23 us
    unnamed x23, local copies, waits for them, and re-layouts  15.7 us
    ppermute x1, waiting for transfers between devices, extended(): before = lax.ppermute(last, axis, up)  14.6 us
    sub x2, other arithmetic, apply_inverse(): fwd_re = values[0] * inv_re - values[1] * inv_im  8.95 us
  transfers between devices with their start and end apart: 3, of which 3 were waited for; matrix products, arithmetic and copies ran while one was open for 2% of the time, Pallas kernels for 0%

commit v1 on v0

--- a/solution.py
+++ b/solution.py
@@ -86,7 +86,9 @@
     summed = jnp.einsum(
         "qkb,kbc->qc",
         weights,
-        lax.all_gather(blocks[None], "shot", axis=0, tiled=True),
+        jnp.concatenate(
+            lax.all_to_all(jnp.stack(lax.axis_size("shot") * [blocks[None]]), "shot", 0, 0), axis=0
+        ),
         precision=lax.Precision.HIGHEST,
     )
     return summed[None]

time: 343 us -> 537 us (1.57)
  waiting for transfers between devices: 211 us -> 401 us
  between operations: 14.2 us -> 0.81 us
  local copies, waits for them, and re-layouts: 28.9 us -> 39.5 us
  starting transfers between devices: 7.77 us -> 15.7 us
    all_to_all x0 -> x1, waiting for transfers between devices: none -> 362 us  [per_device(): lax.all_to_all(jnp.stack(lax.axis_size('shot') * [blocks[None]]), 'shot',...]
    all_gather x1 -> x0, waiting for transfers between devices: 172 us -> none  [per_device(): lax.all_gather(blocks[None], 'shot', axis=0, tiled=True)]
    another operation x0 -> x1, local copies, waits for them, and re-layouts: none -> 11.2 us  [per_device(): jnp.stack(lax.axis_size('shot') * [blocks[None]])]
    all_to_all x0 -> x1, starting transfers between devices: none -> 7.93 us  [per_device(): lax.all_to_all(jnp.stack(lax.axis_size('shot') * [blocks[None]]), 'shot',...]
  transfers between devices with their start and end apart: 3 -> 3, of which waited for: 3 -> 3; matrix products, arithmetic and copies ran while one was open for 2% -> 1% of each run, Pallas kernels for 0% -> 0%
where the time goes in v1:
time: 537 us
  waiting for transfers between devices  401 us (75%)
  other arithmetic  41.9 us (8%)
  local copies, waits for them, and re-layouts  39.5 us (7%)
  matrix products  37.6 us (7%)
  starting transfers between devices  15.7 us (3%)
    all_to_all x1, waiting for transfers between devices, per_device(): lax.all_to_all(jnp.stack(lax.axis_size('shot') * [blocks[None]]), 'shot',...  362 us
    dot_general x1, matrix products, per_device(): jnp.einsum('qkb,kbc->qc', weights, jnp.concatenate(lax.all_to_all(jnp.sta...  37.6 us
    ppermute x1, waiting for transfers between devices, extended(): after = lax.ppermute(first, axis, down)  24.4 us
    add x1, other arithmetic, per_device(): updated = apply_inverse(forcing + neighbours, inv_re, inv_im)  23.1 us
    unnamed x23, local copies, waits for them, and re-layouts  15.1 us
    ppermute x1, waiting for transfers between devices, extended(): before = lax.ppermute(last, axis, up)  14.6 us
    another operation x1, local copies, waits for them, and re-layouts, per_device(): jnp.stack(lax.axis_size('shot') * [blocks[None]])  11.2 us
  transfers between devices with their start and end apart: 3, of which 3 were waited for; matrix products, arithmetic and copies ran while one was open for 1% of the time, Pallas kernels for 0%

profile of v1, /device:TPU:1, one launch (start us, length us, event | category | flops | bytes accessed | tf_op | source)
XLA Modules:
  0.0 536.7 jit_solution(379272933272852218)
XLA Ops:
  0.0 1.2 dynamic_slice.3
  1.9 9.2 %copy.14 = f32[1,2,2,256,8,256]{5,3,4,2,1,0:T(8,128)} copy(f32[1,2,2,256,8,256]{5,4,3,2,1,0:T(8,128)} %param.5) | data formatting | bytes 16777216 | tf_op args[0]
  11.1 5.0 multiply_subtract_fusion.4
  16.2 1.0 maximum_multiply_fusion
  18.8 3.2 copy-done.1
  22.0 1.2 fusion.16
  23.2 6.5 %collective-permute-start = (f32[4,256,1,256]{3,1,2,0:T(8,128)}, f32[4,256,1,256]{3,1,2,0:T(8,128)}, u32[]{:S(2)}, u32[]{:S(2)}) collective-permute-start(f32[4,256,1,256]{3,1,2,0:T(8,128)} %get-tuple-element.13), channel_id=1, source_target_pairs={{0,1},{1,2},{2,3},{3,4},{4,5},{5,6},{6,7},{8,9},{9,10},{10,11},{11... | collective-permute-start | bytes 3145736 | tf_op jit(solution)/shard_map/ppermute | solution.py:18
  29.7 1.3 collective-permute-start.1
  31.1 1.7 broadcast_multiply_fusion
  32.8 3.3 mul.286
  36.1 14.6 %collective-permute-done = f32[4,256,1,256]{3,1,2,0:T(8,128)} collective-permute-done((f32[4,256,1,256]{3,1,2,0:T(8,128)}, f32[4,256,1,256]{3,1,2,0:T(8,128)}, u32[]{:S(2)}, u32[]{:S(2)}) %collective-permute-start) | collective-permute-done | bytes 1048608 | tf_op jit(solution)/shard_map/ppermute | solution.py:18
  50.8 24.4 %collective-permute-done.1 = f32[4,256,1,256]{3,1,2,0:T(8,128)} collective-permute-done((f32[4,256,1,256]{3,1,2,0:T(8,128)S(1)}, f32[4,256,1,256]{3,1,2,0:T(8,128)}, u32[]{:S(2)}, u32[]{:S(2)}) %collective-permute-start.1) | collective-permute-done | bytes 1048608 | tf_op jit(solution)/shard_map/ppermute | solution.py:19
  75.2 23.1 %fusion.5 = f32[4,256,8,256]{3,1,2,0:T(8,128)S(1)} fusion(f32[4,256,8,256]{3,1,2,0:T(8,128)} %copy-done.1, f32[4,256,1,256]{3,1,2,0:T(8,128)} %collective-permute-done.1, f32[4,256,1,256]{3,1,2,0:T(8,128)} %collective-permute-done, f32[1,2,2,256,8,256]{5,3,4,2,1,0:T(8,128)} %copy.14), kind=kLoop, calls=%fused_computation.9 | loop fusion | flops 16777216 | bytes 27262976 | tf_op jit(solution)/shard_map/add | solution.py:67
  98.4 3.9 multiply_subtract_fusion.2
  102.4 1.1 copy-done.7
  103.5 4.2 fusion.8
  108.3 2.5 copy.17
  110.8 3.5 sub.58
  114.3 2.0 mul.287
  116.2 11.2 %stack.8 = f32[16,1,8,65536]{3,2,1,0:T(8,128)} broadcast(f32[8,65536]{1,0:T(8,128)S(1)} %mul.287), dimensions={2,3} | broadcast | bytes 35651584 | tf_op jit(solution)/shard_map/stack | solution.py:90
  127.5 7.9 %all-to-all-start = ((f32[16,1,8,65536]{3,2,1,0:T(8,128)}), f32[16,1,8,65536]{3,2,1,0:T(8,128)}, u32[]{:S(2)}, u32[]{:S(2)}) async-start(f32[16,1,8,65536]{3,2,1,0:T(8,128)} %stack.8), calls=%async_computation | async-start | bytes 67108864 | tf_op jit(solution)/shard_map/all_to_all | solution.py:90
  135.6 1.2 gather_fusion
  137.0 362.2 %all-to-all-done = f32[16,1,8,65536]{3,2,1,0:T(8,128)} async-done(((f32[16,1,8,65536]{3,2,1,0:T(8,128)}), f32[16,1,8,65536]{3,2,1,0:T(8,128)}, u32[]{:S(2)}, u32[]{:S(2)}) %all-to-all-start) | async-done | bytes 33554464 | tf_op jit(solution)/shard_map/all_to_all | solution.py:90
  499.2 37.6 %convolution_bitcast_fusion = f32[1,4,65536]{2,1,0:T(4,128)} fusion(f32[16,1,8,65536]{3,2,1,0:T(8,128)} %all-to-all-done, s32[16,8]{0,1:T(8,128)S(1)} %copy.13, s32[4]{0:T(128)S(1)} %iota_add_fusion.1), kind=kOutput, calls=%fused_computation.1 | convolution fusion | flops 402653696 | bytes 34603536 | tf_op jit(solution)/shard_map/qkb,kbc->qc/dot_general | solution.py:86
  (31 shorter events, 2.6 us)
Async XLA Ops:
  0.0 135.6 %copy-start = (s32[64]{0:T(128)S(1)}, s32[64]{0:T(128)}, u32[]{:S(2)}) copy-start(s32[64]{0:T(128)} %param.9) | copy-start | bytes 772
  16.2 1.5 copy-start.2
  16.2 2.0 copy-start.4
  16.2 2.6 copy-start.6
  18.8 3.2 copy-start.1
  23.2 27.6 %collective-permute-start = (f32[4,256,1,256]{3,1,2,0:T(8,128)}, f32[4,256,1,256]{3,1,2,0:T(8,128)}, u32[]{:S(2)}, u32[]{:S(2)}) collective-permute-start(f32[4,256,1,256]{3,1,2,0:T(8,128)} %get-tuple-element.13), channel_id=1, source_target_pairs={{0,1},{1,2},{2,3},{3,4},{4,5},{5,6},{6,7},{8,9},{9,10},{10,11},{11... | collective-permute-start | bytes 3145736 | tf_op jit(solution)/shard_map/ppermute | solution.py:18
  29.7 45.6 %collective-permute-start.1 = (f32[4,256,1,256]{3,1,2,0:T(8,128)S(1)}, f32[4,256,1,256]{3,1,2,0:T(8,128)}, u32[]{:S(2)}, u32[]{:S(2)}) collective-permute-start(f32[4,256,1,256]{3,1,2,0:T(8,128)S(1)} %get-tuple-element.14), channel_id=1, source_target_pairs={{1,0},{2,1},{3,2},{4,3},{5,4},{6,5},{7,6},{9,8},{10,9},{11,10},{12... | collective-permute-start | bytes 3145736 | tf_op jit(solution)/shard_map/ppermute | solution.py:19
  36.1 62.3 %copy-start.8 = (f32[1,256,8,256]{3,2,1,0:T(8,128)S(1)}, f32[1,256,8,256]{3,2,1,0:T(8,128)}, u32[]{:S(2)}) copy-start(f32[1,256,8,256]{3,2,1,0:T(8,128)} %param.6) | copy-start | bytes 6291460
  98.4 4.0 copy-start.3
  98.4 4.0 copy-start.5
  98.4 5.1 copy-start.7
  110.8 3.5 copy-start.9
  127.5 7.9 %copy-start.10 = (s32[16]{0:T(128)S(1)}, s32[16]{0:T(128)}, u32[]{:S(2)}) copy-start(s32[16]{0:T(128)} %param.8) | copy-start | bytes 196
  127.5 371.7 %all-to-all-start = ((f32[16,1,8,65536]{3,2,1,0:T(8,128)}), f32[16,1,8,65536]{3,2,1,0:T(8,128)}, u32[]{:S(2)}, u32[]{:S(2)}) async-start(f32[16,1,8,65536]{3,2,1,0:T(8,128)} %stack.8), calls=%async_computation | async-start | bytes 67108864 | tf_op jit(solution)/shard_map/all_to_all | solution.py:90
